TPU v7x, 256 devices: a whole 4x4x8 slice. The times are simulated.
256 devices in a mesh: lev: 32 (over y_hi, z, core), pln: 8 (over y_lo, x).
Axes of the slice: x: 4, y: 4 (y_hi: 2, y_lo: 2; y = y_hi * 2 + y_lo), z: 8, core: 2. Of those that a mesh axis runs over, the one named last changes fastest.
Arguments:
- concentration: float32 [128, 1024, 1024], P('lev', 'pln'), may hold values from -2.5 to 2.5
- potential: float32 [1024, 1024], P('pln'), may hold values from -1.5 to 1.5
- lift: float32 [128], replicated, may hold values from 1 to 8
- eigenvalue: float32 [128], replicated, may hold values from 0.05 to 20
- basis: float32 [128, 128], replicated, may hold values from -1 to 2, as said below
- inverse_basis: float32 [128, 128], replicated, may hold values from -1 to 2, as said below
Outputs:
- next_concentration: float32 [128, 1024, 1024], P('lev', 'pln')
Inputs may be any that keep to these rules, and one draw needn't show every extreme that they name: basis times inverse_basis is the identity up to float32 rounding. `inverse_basis`: the matrix inverse of basis, up to float32 rounding.
All inputs are finite; a program needn't handle non-finite values.
Results may differ from a plain program's by a relative error of at most 0.00035.
Values sent between devices are 32-bit elements; how exact they have to be, the bound alone decides.
No kernel may reach another device: no remote copies, remote signals or barrier semaphores. Data moves between devices by JAX's collectives and lax.ppermute only.
A program may use at most 128 MiB of HBM per device.

v0:
```python
import jax
import jax.numpy as jnp
from jax import lax
from jax.sharding import PartitionSpec as P

TIME_STEP = 0.04
GRADIENT_ENERGY = 0.25
EXCHANGE_CURRENT = 0.6


def spread(value, axis, root):
    mine = lax.axis_index(axis) == root
    return lax.psum(jnp.where(mine, value, jnp.zeros_like(value)), axis)


def cas_table(length):
    index = jnp.arange(length, dtype=jnp.int32)
    product = index[:, None] * index[None, :] % length
    angle = product.astype(jnp.float32) * (2.0 * jnp.pi / length)
    return jnp.cos(angle) + jnp.sin(angle)


def wave_squared(index, length):
    folded = jnp.minimum(index, length - index).astype(jnp.float32)
    return (folded * (2.0 * jnp.pi / length)) ** 2


def body(concentration, potential, lift, eigenvalue, basis, inverse_basis):
    highest = lax.Precision.HIGHEST
    lev_count = lax.axis_size("lev")
    pln_count = lax.axis_size("pln")
    lev_index = lax.axis_index("lev")
    pln_index = lax.axis_index("pln")
    own_levels, own_rows, width_y = concentration.shape
    width_x = own_rows * pln_count
    cols_y = width_y // pln_count
    rows_x = width_x // lev_count
    table_x = cas_table(width_x)
    table_y = cas_table(width_y)
    nonlinear = concentration**3 - concentration
    surface = 2.0 * EXCHANGE_CURRENT * jnp.sinh(0.5 * (potential - concentration[0]))
    flux_plane = spread(surface, "lev", 0)
    own_lift = lax.dynamic_slice_in_dim(lift, lev_index * own_levels, own_levels)
    shifted = concentration + TIME_STEP * own_lift[:, None, None] * flux_plane[None]
    stacked = jnp.concatenate([shifted, nonlinear], axis=0)
    along_y = jnp.einsum("lxn,nk->lxk", stacked, table_y, precision=highest)
    spectral = jnp.einsum(
        "kx,lxj->lkj",
        table_x,
        lax.all_to_all(along_y, "pln", split_axis=2, concat_axis=1, tiled=True),
        precision=highest,
    )
    first_modes = spectral[:own_levels]
    second_modes = spectral[own_levels : 2 * own_levels]
    gathered_first, gathered_second = (
        lax.all_to_all(first_modes, "lev", split_axis=1, concat_axis=0, tiled=True),
        lax.all_to_all(second_modes, "lev", split_axis=1, concat_axis=0, tiled=True),
    )
    eigen_first = jnp.einsum("ml,lxy->mxy", inverse_basis, gathered_first, precision=highest)
    eigen_second = jnp.einsum("ml,lxy->mxy", inverse_basis, gathered_second, precision=highest)
    x_index = lev_index * rows_x + jnp.arange(rows_x, dtype=jnp.int32)
    y_index = pln_index * cols_y + jnp.arange(cols_y, dtype=jnp.int32)
    total_wave = wave_squared(x_index, width_x)[:, None] + wave_squared(y_index, width_y)[None, :]
    operator = total_wave[None] + eigenvalue[:, None, None]
    numerator = eigen_first - TIME_STEP * operator * eigen_second
    update = numerator / (1.0 + TIME_STEP * GRADIENT_ENERGY * operator * operator)
    level_values = jnp.einsum("lm,mxy->lxy", basis, update, precision=highest)
    returned = lax.all_to_all(level_values, "lev", split_axis=0, concat_axis=1, tiled=True)
    back_x = jnp.einsum("kx,lxj->lkj", table_x, returned, precision=highest)
    scale_factor = 1.0 / (width_x * width_y)
    return (
        jnp.einsum(
            "lxn,nk->lxk",
            lax.all_to_all(back_x, "pln", split_axis=1, concat_axis=2, tiled=True),
            table_y,
            precision=highest,
        )
        * scale_factor
    )


def solution(mesh):
    in_specs = (P("lev", "pln", None), P("pln", None), P(), P(), P(), P())
    out_specs = P("lev", "pln", None)
    return jax.shard_map(body, mesh=mesh, in_specs=in_specs, out_specs=out_specs, check_vma=False)
```

profile of v0, /device:TPU:32, one launch (start us, length us, event | category | flops | bytes accessed | tf_op | source)
XLA Modules:
  0.0 676.0 jit_solution(15718346257006392588)
XLA Ops:
  6.5 2.5 fusion.47
  9.8 266.7 %all-reduce.2.cloned.1.call-done = f32[128,1024]{1,0:T(8,128)} async-done(((f32[128,1024]{1,0:T(8,128)}), f32[128,1024]{1,0:T(8,128)}) %all-reduce.2.cloned.1.call-update) | async-done | bytes 524304 | tf_op jit(solution)/shard_map/psum | solution.py:13
  276.5 2.2 multiply_add_fusion
  279.3 31.3 %fusion.3 = f32[8,128,1024]{2,1,0:T(8,128)} fusion(f32[8,128,1024]{2,1,0:T(8,128)S(1)} %fusion.97), kind=kOutput, calls=%fused_computation.6 | convolution fusion | flops 12900630528 | bytes 8388608 | tf_op jit(solution)/shard_map/lxn,nk->lxk/dot_general | solution.py:46
  310.6 5.4 copy.19
  315.9 4.9 all-to-all-start
  320.9 17.5 %fusion.99 = f32[1024,1024,1]{1,0,2:T(8,128)} fusion(), kind=kLoop, calls=%fused_computation.15.clone.clone.clone.1 | loop fusion | flops 15728640 | bytes 4194304 | tf_op jit(solution)/shard_map/kx,lxj->lkj/dot_general | solution.py:47
  338.4 32.4 %all-to-all-done = f32[8,128,1024]{1,0,2:T(8,128)} async-done(((f32[8,128,1024]{1,0,2:T(8,128)}), f32[8,128,1024]{1,0,2:T(8,128)}, u32[]{:S(2)}, u32[]{:S(2)}) %all-to-all-start) | async-done | bytes 4194336 | tf_op jit(solution)/shard_map/all_to_all | solution.py:50
  370.8 6.6 copy.41
  377.4 4.9 all_to_all.68
  382.3 16.9 %fusion.17 = f32[8,1024,128]{1,2,0:T(8,128)S(1)} fusion(f32[8,1024,128]{1,2,0:T(8,128)} %all_to_all.68, f32[1024,1024,1]{1,0,2:T(8,128)} %fusion.99), kind=kOutput, calls=%fused_computation.26 | convolution fusion | flops 12884901888 | bytes 12582912 | tf_op jit(solution)/shard_map/kx,lxj->lkj/dot_general | solution.py:47
  401.0 1.8 copy.25
  402.8 9.3 %all-to-all-start.2 = ((f32[4,1024,128]{2,0,1:T(4,128)}), f32[4,1024,128]{2,0,1:T(4,128)S(1)}, u32[]{:S(2)}, u32[]{:S(2)}) async-start(f32[4,1024,128]{2,0,1:T(4,128)} %copy.25), calls=%async_computation.2 | async-start | bytes 4194304 | tf_op jit(solution)/shard_map/all_to_all | solution.py:57
  412.1 2.9 copy.21
  415.0 50.1 %all-to-all-done.2 = f32[4,1024,128]{2,0,1:T(4,128)S(1)} async-done(((f32[4,1024,128]{2,0,1:T(4,128)}), f32[4,1024,128]{2,0,1:T(4,128)S(1)}, u32[]{:S(2)}, u32[]{:S(2)}) %all-to-all-start.2) | async-done | bytes 2097184 | tf_op jit(solution)/shard_map/all_to_all | solution.py:57
  465.1 4.6 all-to-all-start.1
  470.2 51.6 %all-to-all-done.1 = f32[4,1024,128]{2,0,1:T(4,128)} async-done(((f32[4,1024,128]{2,0,1:T(4,128)}), f32[4,1024,128]{2,0,1:T(4,128)}, u32[]{:S(2)}, u32[]{:S(2)}) %all-to-all-start.1) | async-done | bytes 2097184 | tf_op jit(solution)/shard_map/all_to_all | solution.py:56
  523.7 4.3 fusion.24
  528.0 4.3 fusion.26
  532.3 2.2 fusion.30
  534.6 2.1 copy.29
  536.7 3.8 all-to-all-start.3
  540.5 17.5 %fusion.101 = f32[1024,1024,1]{1,0,2:T(8,128)} fusion(), kind=kLoop, calls=%fused_computation.13.clone.clone.clone.1 | loop fusion | flops 15728640 | bytes 4194304 | tf_op jit(solution)/shard_map/kx,lxj->lkj/dot_general | solution.py:69
  558.0 35.1 %all-to-all-done.3 = f32[128,32,128]{2,1,0:T(8,128)S(1)} async-done(((f32[128,32,128]{2,1,0:T(8,128)}), f32[128,32,128]{2,1,0:T(8,128)S(1)}, u32[]{:S(2)}, u32[]{:S(2)}) %all-to-all-start.3) | async-done | bytes 2097184 | tf_op jit(solution)/shard_map/all_to_all | solution.py:68
  593.3 2.0 copy-done.1
  595.3 13.7 %fusion.33 = f32[4,1024,128]{1,2,0:T(8,128)S(1)} fusion(f32[4,1024,128]{2,1,0:T(8,128)S(1)} %bitcast.103, f32[1024,1024,1]{1,0,2:T(8,128)S(1)} %copy-done.1), kind=kOutput, calls=%fused_computation.39 | convolution fusion | flops 6442450944 | bytes 8388608 | tf_op jit(solution)/shard_map/kx,lxj->lkj/dot_general | solution.py:69
  609.0 1.8 copy.32
  610.8 17.6 %all-to-all-start.4 = ((f32[4,1024,128]{2,0,1:T(4,128)}), f32[4,1024,128]{2,0,1:T(4,128)S(1)}, u32[]{:S(2)}, u32[]{:S(2)}) async-start(f32[4,1024,128]{2,0,1:T(4,128)} %copy.32), calls=%async_computation.4 | async-start | bytes 4194304 | tf_op jit(solution)/shard_map/all_to_all | solution.py:74
  628.4 17.5 %fusion.103 = f32[1024,1024,1]{1,0,2:T(8,128)} fusion(), kind=kLoop, calls=%fused_computation.11.clone.clone.clone.1 | loop fusion | flops 15728640 | bytes 4194304 | tf_op jit(solution)/shard_map/lxn,nk->lxk/dot_general | solution.py:72
  645.9 9.1 %all-to-all-done.4 = f32[4,1024,128]{2,0,1:T(4,128)S(1)} async-done(((f32[4,1024,128]{2,0,1:T(4,128)}), f32[4,1024,128]{2,0,1:T(4,128)S(1)}, u32[]{:S(2)}, u32[]{:S(2)}) %all-to-all-start.4) | async-done | bytes 2097184 | tf_op jit(solution)/shard_map/all_to_all | solution.py:74
  655.0 2.5 copy.42
  659.3 9.6 %fusion.36 = f32[4,128,1024]{2,1,0:T(8,128)} fusion(f32[4,128,1024]{2,1,0:T(8,128)S(1)} %all_to_all.84, f32[1024,1024,1]{1,0,2:T(8,128)} %fusion.103), kind=kOutput, calls=%fused_computation.40 | convolution fusion | flops 6442975232 | bytes 8388608 | tf_op jit(solution)/shard_map/lxn,nk->lxk/dot_general | solution.py:72
  (21 shorter events, 7.4 us)
Async XLA Ops:
  6.5 517.2 %copy-start = (f32[128,128]{1,0:T(8,128)S(1)}, f32[128,128]{1,0:T(8,128)}, u32[]{:S(2)}) copy-start(f32[128,128]{1,0:T(8,128)} %param.11) | copy-start | bytes 196612
  6.5 269.9 %all-reduce.2.cloned.1.call-start = ((), (), s32[]{:S(2)}) async-start(), calls=%async_computation.5 | async-start | bytes 1048576 | tf_op jit(solution)/shard_map/psum | solution.py:13
  315.9 54.8 %all-to-all-start = ((f32[8,128,1024]{1,0,2:T(8,128)}), f32[8,128,1024]{1,0,2:T(8,128)}, u32[]{:S(2)}, u32[]{:S(2)}) async-start(f32[8,128,1024]{1,0,2:T(8,128)} %copy.19), calls=%async_computation | async-start | bytes 8388608 | tf_op jit(solution)/shard_map/all_to_all | solution.py:50
  402.8 62.3 %all-to-all-start.2 = ((f32[4,1024,128]{2,0,1:T(4,128)}), f32[4,1024,128]{2,0,1:T(4,128)S(1)}, u32[]{:S(2)}, u32[]{:S(2)}) async-start(f32[4,1024,128]{2,0,1:T(4,128)} %copy.25), calls=%async_computation.2 | async-start | bytes 4194304 | tf_op jit(solution)/shard_map/all_to_all | solution.py:57
  465.1 56.6 %all-to-all-start.1 = ((f32[4,1024,128]{2,0,1:T(4,128)}), f32[4,1024,128]{2,0,1:T(4,128)}, u32[]{:S(2)}, u32[]{:S(2)}) async-start(f32[4,1024,128]{2,0,1:T(4,128)} %copy.21), calls=%async_computation.1 | async-start | bytes 4194304 | tf_op jit(solution)/shard_map/all_to_all | solution.py:56
  523.7 8.6 %copy-start.2 = (f32[128,128]{1,0:T(8,128)S(1)}, f32[128,128]{1,0:T(8,128)}, u32[]{:S(2)}) copy-start(f32[128,128]{1,0:T(8,128)} %param.10) | copy-start | bytes 196612
  523.7 8.6 %copy-start.3 = (f32[128]{0:T(128)S(1)}, f32[128]{0:T(128)}, u32[]{:S(2)}) copy-start(f32[128]{0:T(128)} %param.9) | copy-start | bytes 1540
  536.7 56.4 %all-to-all-start.3 = ((f32[128,32,128]{2,1,0:T(8,128)}), f32[128,32,128]{2,1,0:T(8,128)S(1)}, u32[]{:S(2)}, u32[]{:S(2)}) async-start(f32[128,32,128]{2,1,0:T(8,128)} %copy.29), calls=%async_computation.3 | async-start | bytes 4194304 | tf_op jit(solution)/shard_map/all_to_all | solution.py:68
  593.1 2.2 copy-start.1
  610.8 44.2 %all-to-all-start.4 = ((f32[4,1024,128]{2,0,1:T(4,128)}), f32[4,1024,128]{2,0,1:T(4,128)S(1)}, u32[]{:S(2)}, u32[]{:S(2)}) async-start(f32[4,1024,128]{2,0,1:T(4,128)} %copy.32), calls=%async_computation.4 | async-start | bytes 4194304 | tf_op jit(solution)/shard_map/all_to_all | solution.py:74
Sparse Core Ops, SparseCore 0:
  9.9 266.4 all-reduce.1
where the time goes:
time: 684 us; the launch traced here: 676 us
  waiting for transfers between devices  445 us (65%)
  matrix products  82.2 us (12%)
  other arithmetic  58.7 us (9%)
  starting transfers between devices  40.1 us (6%)
  local copies, waits for them, and re-layouts  36.1 us (5%)
  between operations  13.8 us (2%)
    psum x1, waiting for transfers between devices, spread(): return lax.psum(jnp.where(mine, value, jnp.zeros_like(value)), axis)  267 us
    all_to_all x1, waiting for transfers between devices, body(): lax.all_to_all(first_modes, 'lev', split_axis=1, concat_axis=0, tiled=True)  51.6 us
    all_to_all x1, waiting for transfers between devices, body(): lax.all_to_all(second_modes, 'lev', split_axis=1, concat_axis=0, tiled=True)  50.1 us
    all_to_all x1, waiting for transfers between devices, body(): lax.all_to_all(level_values, 'lev', split_axis=0, concat_axis=1, tiled=True)  35.1 us
    all_to_all x1, waiting for transfers between devices, body(): lax.all_to_all(along_y, 'pln', split_axis=2, concat_axis=1, tiled=True)  32.4 us
    dot_general x1, matrix products, body(): along_y = jnp.einsum('lxn,nk->lxk', stacked, table_y, precision=highest)  31.3 us
    all_to_all x1, starting transfers between devices, body(): lax.all_to_all(back_x, 'pln', split_axis=1, concat_axis=2, tiled=True)  17.6 us
    dot_general x1, other arithmetic, body(): back_x = jnp.einsum('kx,lxj->lkj', table_x, returned, precision=highest)  17.5 us
  transfers between devices with their start and end apart: 6, of which 6 were waited for; matrix products, arithmetic and copies ran while one was open for 8% of the time, Pallas kernels for 0%

commit v1 on v0

v1 whole, which is shorter than its diff:
```python
import math

import jax
import jax.numpy as jnp
from jax import lax
from jax.sharding import PartitionSpec as P

TIME_STEP = 0.04
GRADIENT_ENERGY = 0.25
EXCHANGE_CURRENT = 0.6


def cas_table(length):
    index = jnp.arange(length, dtype=jnp.int32)
    product = index[:, None] * index[None, :] % length
    angle = product.astype(jnp.float32) * (2.0 * jnp.pi / length)
    return math.sqrt(2.0) * jnp.sin(angle + 0.25 * jnp.pi)


def wave_squared(index, length):
    folded = jnp.minimum(index, length - index).astype(jnp.float32)
    return (folded * (2.0 * jnp.pi / length)) ** 2


def body(concentration, potential, lift, eigenvalue, basis, inverse_basis):
    highest = lax.Precision.HIGHEST
    fast = lax.Precision.HIGH
    lev_count = lax.axis_size("lev")
    pln_count = lax.axis_size("pln")
    lev_index = lax.axis_index("lev")
    pln_index = lax.axis_index("pln")
    own_levels, own_rows, width_y = concentration.shape
    width_x = own_rows * pln_count
    cols_y = width_y // pln_count
    rows_x = width_x // lev_count
    table_y = lax.optimization_barrier(cas_table(width_y))
    table_x = table_y if width_x == width_y else lax.optimization_barrier(cas_table(width_x))
    nonlinear = concentration**3 - concentration
    surface = 2.0 * EXCHANGE_CURRENT * jnp.sinh(0.5 * (potential - concentration[0]))
    stacked = jnp.concatenate([concentration, nonlinear, surface[None]], axis=0)
    along_y = jnp.einsum("lxn,nk->lxk", stacked, table_y, precision=fast)
    spectral = jnp.einsum(
        "kx,lxj->lkj",
        table_x,
        lax.all_to_all(along_y, "pln", split_axis=2, concat_axis=1, tiled=True),
        precision=fast,
    )
    first_modes = jnp.concatenate([spectral[:own_levels], spectral[2 * own_levels :]], axis=0)
    second_modes = spectral[own_levels : 2 * own_levels]
    gathered_first = lax.all_to_all(first_modes, "lev", split_axis=1, concat_axis=0, tiled=True)
    gathered_second = lax.all_to_all(second_modes, "lev", split_axis=1, concat_axis=0, tiled=True)
    gathered_first = gathered_first.reshape(lev_count, own_levels + 1, rows_x, cols_y)
    conc_modes = gathered_first[:, :own_levels].reshape(lev_count * own_levels, rows_x, cols_y)
    surface_modes = gathered_first[0, own_levels]
    lift_weight = jnp.einsum("ml,l->m", inverse_basis, lift, precision=highest)
    eigen_first = (
        jnp.einsum("ml,lxy->mxy", inverse_basis, conc_modes, precision=highest)
        + TIME_STEP * lift_weight[:, None, None] * surface_modes[None]
    )
    eigen_second = jnp.einsum("ml,lxy->mxy", inverse_basis, gathered_second, precision=highest)
    x_index = lev_index * rows_x + jnp.arange(rows_x, dtype=jnp.int32)
    y_index = pln_index * cols_y + jnp.arange(cols_y, dtype=jnp.int32)
    total_wave = wave_squared(x_index, width_x)[:, None] + wave_squared(y_index, width_y)[None, :]
    operator = total_wave[None] + eigenvalue[:, None, None]
    numerator = eigen_first - TIME_STEP * operator * eigen_second
    update = numerator / (1.0 + TIME_STEP * GRADIENT_ENERGY * operator * operator)
    level_values = jnp.einsum("lm,mxy->lxy", basis, update, precision=highest)
    returned = lax.all_to_all(level_values, "lev", split_axis=0, concat_axis=1, tiled=True)
    back_x = jnp.einsum("kx,lxj->lkj", table_x, returned, precision=fast)
    scale_factor = 1.0 / (width_x * width_y)
    return (
        jnp.einsum(
            "lxn,nk->lxk",
            lax.all_to_all(back_x, "pln", split_axis=1, concat_axis=2, tiled=True),
            table_y,
            precision=fast,
        )
        * scale_factor
    )


def solution(mesh):
    in_specs = (P("lev", "pln", None), P("pln", None), P(), P(), P(), P())
    out_specs = P("lev", "pln", None)
    return jax.shard_map(body, mesh=mesh, in_specs=in_specs, out_specs=out_specs, check_vma=False)
```

time: 684 us -> 463 us (0.68)
  waiting for transfers between devices: 445 us -> 135 us
  blocking collectives: 0 us -> 190 us
  other arithmetic: 58.7 us -> 18.7 us
  matrix products: 82.2 us -> 48.9 us
  starting transfers between devices: 40.1 us -> 16.1 us
  between operations: 13.8 us -> 0.66 us
  local copies, waits for them, and re-layouts: 36.1 us -> 43.3 us
    psum x1 -> x0, waiting for transfers between devices: 267 us -> none  [spread(): return lax.psum(jnp.where(mine, value, jnp.zeros_like(value)), axis)]
    all_to_all x0 -> x3, blocking collectives: none -> 190 us  [the longest x1 101 us: body(): lax.all_to_all(along_y, 'pln', split_axis=2, concat_axis=1, tiled=True)]
    all_to_all x3 -> x0, waiting for transfers between devices: 76.6 us -> none  [the longest x1 35.1 us: body(): lax.all_to_all(level_values, 'lev', split_axis=0, concat_axis=1, tiled=True)]
    dot_general x4 -> x0, other arithmetic: 53.1 us -> none  [the longest x1 17.5 us: body(): back_x = jnp.einsum('kx,lxj->lkj', table_x, returned, precision=highest)]
    all_to_all x1, waiting for transfers between devices: 51.6 us -> 87.6 us  [body(): lax.all_to_all(first_modes, 'lev', split_axis=1, concat_axis=0, tiled=True)]
    dot_general x3 -> x4, matrix products: 49.2 us -> 22.3 us  [the longest x1 9.69 us: body(): along_y = jnp.einsum('lxn,nk->lxk', stacked, table_y, precision=fast)]
    all_to_all x3 -> x0, starting transfers between devices: 26.3 us -> none  [the longest x1 17.6 us: body(): lax.all_to_all(back_x, 'pln', split_axis=1, concat_axis=2, tiled=True)]
    mul x1, other arithmetic: 0.73 us -> 16 us  [cas_table(): return math.sqrt(2.0) * jnp.sin(angle + 0.25 * jnp.pi)]
  transfers between devices with their start and end apart: 6 -> 2, of which waited for: 6 -> 2; matrix products, arithmetic and copies ran while one was open for 8% -> 3% of each run, Pallas kernels for 0% -> 0%
where the time goes in v1:
time: 463 us; the launch traced here: 453 us
  blocking collectives  190 us (41%)
  waiting for transfers between devices  135 us (29%)
  matrix products  48.9 us (11%)
  local copies, waits for them, and re-layouts  43.3 us (9%)
  other arithmetic  18.7 us (4%)
  starting transfers between devices  16.1 us (3%)
    all_to_all x1, blocking collectives, body(): lax.all_to_all(along_y, 'pln', split_axis=2, concat_axis=1, tiled=True)  101 us
    all_to_all x1, waiting for transfers between devices, body(): lax.all_to_all(first_modes, 'lev', split_axis=1, concat_axis=0, tiled=True)  87.6 us
    all_to_all x1, blocking collectives, body(): lax.all_to_all(level_values, 'lev', split_axis=0, concat_axis=1, tiled=True)  61.1 us
    all_to_all x1, waiting for transfers between devices, body(): lax.all_to_all(second_modes, 'lev', split_axis=1, concat_axis=0, tiled=True)  47.7 us
    all_to_all x1, blocking collectives, body(): lax.all_to_all(back_x, 'pln', split_axis=1, concat_axis=2, tiled=True)  28.5 us
    mul x1, other arithmetic, cas_table(): return math.sqrt(2.0) * jnp.sin(angle + 0.25 * jnp.pi)  16 us
    all_to_all x1, starting transfers between devices, body(): lax.all_to_all(second_modes, 'lev', split_axis=1, concat_axis=0, tiled=True)  11.3 us
    all_to_all x2, local copies, waits for them, and re-layouts, body(): lax.all_to_all(along_y, 'pln', split_axis=2, concat_axis=1, tiled=True)  10.8 us
  transfers between devices with their start and end apart: 2, of which 2 were waited for; matrix products, arithmetic and copies ran while one was open for 3% of the time, Pallas kernels for 0%

profile of v1, /device:TPU:32, one launch (start us, length us, event | category | flops | bytes accessed | tf_op | source)
XLA Modules:
  0.0 453.5 jit_solution(10036693752472993962)
XLA Ops:
  0.0 16.0 %fusion.11 = f32[1024,1024]{1,0:T(8,128)S(1)} fusion(), kind=kLoop, calls=%fused_computation.15 | loop fusion | flops 16777216 | bytes 4194304 | tf_op jit(solution)/shard_map/mul | solution.py:17
  16.4 1.0 copy-done.5
  17.4 0.5 fusion.55
  17.9 9.7 %fusion = f32[9,128,1024]{2,1,0:T(8,128)} fusion(f32[1,128,1024]{2,1,0:T(8,128)S(1)} %fusion.55, f32[4,128,1024]{2,1,0:T(8,128)S(1)} %multiply_subtract_fusion, f32[4,128,1024]{2,1,0:T(8,128)S(1)} %copy-done.4, f32[1024,1024]{1,0:T(8,128)S(1)} %fusion.11), kind=kOutput, calls=%fused_computation.3 | convolution fusion | flops 7250116608 | bytes 13631488 | tf_op jit(solution)/shard_map/lxn,nk->lxk/dot_general | solution.py:41
  27.6 9.0 %copy.20 = f32[9,128,1024]{1,0,2:T(8,128)} copy(f32[9,128,1024]{2,1,0:T(8,128)} %fusion) | data formatting | bytes 9437184 | tf_op jit(solution)/shard_map/lxn,nk->lxk/dot_general | solution.py:41
  36.6 100.7 %all_to_all.87 = f32[9,128,1024]{1,0,2:T(8,128)S(1)} all-to-all(f32[9,128,1024]{1,0,2:T(8,128)} %copy.20), channel_id=1, replica_groups=mesh['lev'=32,'pln'=8] {'pln'}, dimensions={2} | all-to-all | bytes 9437184 | tf_op jit(solution)/shard_map/all_to_all | solution.py:45
  137.3 4.9 %copy.42 = f32[9,128,8,128]{1,2,3,0:T(8,128)} copy(f32[9,128,8,128]{1,0,3,2:T(8,128)S(1)} %bitcast.88) | data formatting | bytes 9437184 | tf_op jit(solution)/shard_map/all_to_all | solution.py:45
  142.2 6.0 %all_to_all.66 = f32[9,1024,128]{1,2,0:T(8,128)} reshape(f32[9,8,128,128]{2,1,3,0:T(8,128)} %bitcast.89) | data formatting | bytes 9437184 | tf_op jit(solution)/shard_map/all_to_all | solution.py:45
  148.2 10.8 %fusion.22 = f32[9,1024,128]{1,2,0:T(8,128)S(1)} fusion(f32[9,1024,128]{1,2,0:T(8,128)} %all_to_all.66, f32[1024,1024]{1,0:T(8,128)} %copy-done.1), kind=kOutput, calls=%fused_computation.31 | convolution fusion | flops 7247757312 | bytes 13631488 | tf_op jit(solution)/shard_map/kx,lxj->lkj/dot_general | solution.py:42
  158.9 2.0 fusion.71
  160.9 0.8 copy-done.3
  161.7 1.8 copy.26
  163.6 11.3 %all-to-all-start.2 = ((f32[4,1024,128]{2,0,1:T(4,128)}), f32[4,1024,128]{2,0,1:T(4,128)}, u32[]{:S(2)}, u32[]{:S(2)}) async-start(f32[4,1024,128]{2,0,1:T(4,128)} %copy.26), calls=%async_computation.2 | async-start | bytes 4194304 | tf_op jit(solution)/shard_map/all_to_all | solution.py:51
  174.8 1.8 pad_maximum_fusion
  176.6 3.5 copy.22
  180.1 47.7 %all-to-all-done.2 = f32[4,1024,128]{2,0,1:T(4,128)} async-done(((f32[4,1024,128]{2,0,1:T(4,128)}), f32[4,1024,128]{2,0,1:T(4,128)}, u32[]{:S(2)}, u32[]{:S(2)}) %all-to-all-start.2) | async-done | bytes 2097184 | tf_op jit(solution)/shard_map/all_to_all | solution.py:51
  227.8 4.9 %all-to-all-start.1 = ((f32[5,1024,128]{2,0,1:T(8,128)}), f32[5,1024,128]{2,0,1:T(8,128)}, u32[]{:S(2)}, u32[]{:S(2)}) async-start(f32[5,1024,128]{2,0,1:T(8,128)} %copy.22), calls=%async_computation.1 | async-start | bytes 8388608 | tf_op jit(solution)/shard_map/all_to_all | solution.py:50
  233.0 1.8 copy.27
  235.0 4.2 fusion.29
  239.3 87.6 %all-to-all-done.1 = f32[5,1024,128]{2,0,1:T(8,128)} async-done(((f32[5,1024,128]{2,0,1:T(8,128)}), f32[5,1024,128]{2,0,1:T(8,128)}, u32[]{:S(2)}, u32[]{:S(2)}) %all-to-all-start.1) | async-done | bytes 2621472 | tf_op jit(solution)/shard_map/all_to_all | solution.py:50
  326.9 2.7 copy.23
  330.0 4.3 fusion.31
  334.4 3.9 fusion.35
  338.3 2.4 copy.30
  340.7 61.1 %all_to_all.88 = f32[128,32,128]{2,1,0:T(8,128)S(1)} all-to-all(f32[128,32,128]{2,1,0:T(8,128)S(1)} %copy.30), channel_id=1, replica_groups=mesh['lev'=32,'pln'=8] {'lev'}, dimensions={0} | all-to-all | bytes 4194304 | tf_op jit(solution)/shard_map/all_to_all | solution.py:68
  401.9 2.0 copy-done.2
  404.0 8.2 %fusion.38 = f32[4,1024,128]{1,2,0:T(8,128)} fusion(f32[4,1024,128]{2,1,0:T(8,128)S(1)} %bitcast.98, f32[1024,1024]{1,0:T(8,128)S(1)} %copy-done.2), kind=kOutput, calls=%fused_computation.44 | convolution fusion | flops 3221225472 | bytes 8388608 | tf_op jit(solution)/shard_map/kx,lxj->lkj/dot_general | solution.py:69
  412.1 2.0 copy.33
  414.1 28.5 %all_to_all.89 = f32[4,1024,128]{2,0,1:T(4,128)S(1)} all-to-all(f32[4,1024,128]{2,0,1:T(4,128)S(1)} %copy.33), channel_id=1, replica_groups=mesh['lev'=32,'pln'=8] {'pln'}, dimensions={1} | all-to-all | bytes 4194304 | tf_op jit(solution)/shard_map/all_to_all | solution.py:74
  442.6 1.2 copy.43
  443.9 1.5 all_to_all.81
  445.4 7.7 %fusion.41 = f32[4,128,1024]{2,1,0:T(8,128)} fusion(f32[4,128,1024]{2,1,0:T(8,128)} %all_to_all.81, f32[1024,1024]{1,0:T(8,128)} %copy-done.1), kind=kOutput, calls=%fused_computation.45 | convolution fusion | flops 3221749760 | bytes 8388608 | tf_op jit(solution)/shard_map/lxn,nk->lxk/dot_general | solution.py:72
  (27 shorter events, 1.6 us)
Async XLA Ops:
  0.0 232.8 %copy-start = (f32[128,128]{1,0:T(8,128)S(1)}, f32[128,128]{1,0:T(8,128)}, u32[]{:S(2)}) copy-start(f32[128,128]{1,0:T(8,128)} %param.11) | copy-start | bytes 196612
  0.0 16.0 %copy-start.4 = (f32[4,128,1024]{2,1,0:T(8,128)S(1)}, f32[4,128,1024]{2,1,0:T(8,128)}, u32[]{:S(2)}) copy-start(f32[4,128,1024]{2,1,0:T(8,128)} %param.6) | copy-start | bytes 6291460
  16.0 1.9 copy-start.1
  16.0 1.4 copy-start.5
  158.9 2.8 copy-start.3
  163.6 11.3 %slice-start = ((f32[9,1024,128]{1,2,0:T(8,128)}), f32[1,1024,128]{1,2,0:T(8,128)S(1)}, s32[]{:S(2)}) async-start(f32[9,1024,128]{1,2,0:T(8,128)} %copy-done.3), calls=%async_computation.5 | async-start | bytes 1048576 | tf_op jit(solution)/shard_map/slice | solution.py:48
  163.6 64.2 %all-to-all-start.2 = ((f32[4,1024,128]{2,0,1:T(4,128)}), f32[4,1024,128]{2,0,1:T(4,128)}, u32[]{:S(2)}, u32[]{:S(2)}) async-start(f32[4,1024,128]{2,0,1:T(4,128)} %copy.26), calls=%async_computation.2 | async-start | bytes 4194304 | tf_op jit(solution)/shard_map/all_to_all | solution.py:51
  180.1 52.7 %copy-start.6 = (f32[128]{0:T(128)S(1)}, f32[128]{0:T(128)}, u32[]{:S(2)}) copy-start(f32[128]{0:T(128)} %param.8) | copy-start | bytes 1540
  227.8 99.1 %all-to-all-start.1 = ((f32[5,1024,128]{2,0,1:T(8,128)}), f32[5,1024,128]{2,0,1:T(8,128)}, u32[]{:S(2)}, u32[]{:S(2)}) async-start(f32[5,1024,128]{2,0,1:T(8,128)} %copy.22), calls=%async_computation.1 | async-start | bytes 8388608 | tf_op jit(solution)/shard_map/all_to_all | solution.py:50
  330.0 4.3 copy-start.7
  330.0 4.3 copy-start.8
  401.8 2.2 copy-start.2
